TPU v7x, 32 devices: a whole 2x2x4 slice. The times are simulated.
32 devices in a mesh: ctx: 16 (over z, y, x), head: 2 (over core).
Axes of the slice: x: 2, y: 2, z: 4, core: 2. Of those that a mesh axis runs over, the one named last changes fastest.
Arguments:
- queries: bfloat16 [4096, 4096], P('ctx', 'head')
- keys: bfloat16 [4096, 1024], P('ctx', 'head')
- values: bfloat16 [4096, 1024], P('ctx', 'head'), may hold values from -6 to 6
- positions: int32 [4096], P('ctx'), may hold values from 0 to 6143, as said below
- retrieval: int32 [4], replicated, may hold values from 0 to 7, as said below
- yarn_scale: int32 [1], replicated, may hold values from 2 to 8
- out_weight: bfloat16 [4096, 4096], P('head', 'ctx'), may hold values from -0.125 to 0.125
Outputs:
- layer_out: bfloat16 [4096, 4096], P('ctx', 'head')
Inputs may be any that keep to these rules, and one draw needn't show every extreme that they name: positions start at 0 and rise by 1 or 2 from one token to the next, by 2 at exactly 2048 of the steps. `retrieval`: 4 different KV-head indices.
All inputs are finite; a program needn't handle non-finite values.
Results may differ from a plain program's by a relative error of at most 0.014.
The roundings to bfloat16 on the way count: a program that leaves them out, or rounds other values in their place, can miss the bound.
Values may be sent and summed in bfloat16 or wider, within the bound.
No kernel may reach another device: no remote copies, remote signals or barrier semaphores. Data moves between devices by JAX's collectives and lax.ppermute only.
A program may use at most 128 MiB of HBM per device.

v0:
```python
from functools import partial
import math
import jax
import jax.numpy as jnp
from jax import lax
from jax.sharding import PartitionSpec as P

HEAD_SIZE = 128
SINK = 64
WINDOW = 256
ORIG_CTX = 8192
QUERY_PER_KEY = 4
rope_base = 500000.0
neg_big = -1e30


def yarn_tables(positions, yarn_scale):
    half_size = HEAD_SIZE // 2
    factor = yarn_scale[0].astype(jnp.float32)
    freq_index = jnp.arange(half_size, dtype=jnp.float32)
    base_freq = jnp.power(jnp.float32(rope_base), -2.0 * freq_index / HEAD_SIZE)
    wave_ratio = ORIG_CTX * base_freq / (2.0 * math.pi)
    ramp_weight = jnp.clip((wave_ratio - 1.0) / 31.0, 0.0, 1.0)
    yarn_freq = base_freq * ramp_weight + base_freq / factor * (1.0 - ramp_weight)
    angles = positions.astype(jnp.float32)[:, None] * yarn_freq[None, :]
    mscale = 0.1 * jnp.log(factor) + 1.0
    return (jnp.cos(angles) * mscale, jnp.sin(angles) * mscale)


def apply_rotary(x, cosine_lookup, sine_lookup, head_count):
    row_count = x.shape[0]
    shaped = x.astype(jnp.float32).reshape(row_count, head_count, HEAD_SIZE)
    lower_half = shaped[..., : HEAD_SIZE // 2]
    upper_half = shaped[..., HEAD_SIZE // 2 :]
    cosine = cosine_lookup[:, None, :]
    sine_part = sine_lookup[:, None, :]
    rotated = jnp.concatenate(
        [
            lower_half * cosine - upper_half * sine_part,
            upper_half * cosine + lower_half * sine_part,
        ],
        axis=-1,
    )
    return rotated.reshape(row_count, head_count * HEAD_SIZE).astype(jnp.bfloat16)


def update(query_rows, key_block, value_block, visible, partial_state):
    row_max, totals, accum = partial_state
    scores = jnp.einsum(
        "rhgd,khd->hgrk", query_rows, key_block, preferred_element_type=jnp.float32
    ) * (1.0 / math.sqrt(HEAD_SIZE))
    mask_full = visible[:, None]
    scores = jnp.where(mask_full, scores, neg_big)
    new_max = jnp.maximum(row_max, jnp.max(scores, axis=-1))
    weights = jnp.where(mask_full, jnp.exp(scores - new_max[..., None]), 0.0)
    rescale = jnp.exp(row_max - new_max)
    totals = totals * rescale + jnp.sum(weights, axis=-1)
    accum = accum * rescale[..., None] + jnp.einsum(
        "hgrk,khd->hgrd",
        weights.astype(jnp.bfloat16),
        value_block,
        preferred_element_type=jnp.float32,
    )
    return (new_max, totals, accum)


def attend(query_sets, rotated_key, values, flags, kv_local):
    shaped_sets = []
    initial = []
    for query_rows, query_index in query_sets:
        row_count = query_rows.shape[0]
        shaped_sets.append(
            (query_rows.reshape(row_count, kv_local, QUERY_PER_KEY, HEAD_SIZE), query_index)
        )
        initial.append(
            (
                jnp.full((kv_local, QUERY_PER_KEY, row_count), neg_big, jnp.float32),
                jnp.zeros((kv_local, QUERY_PER_KEY, row_count), jnp.float32),
                jnp.zeros((kv_local, QUERY_PER_KEY, row_count, HEAD_SIZE), jnp.float32),
            )
        )
    initial = tuple(initial)
    key_shard = lax.all_gather(rotated_key, "ctx", axis=0, tiled=True)
    value_shard = lax.all_gather(values, "ctx", axis=0, tiled=True)
    shard_rows = key_shard.shape[0]
    sub_rows = math.gcd(shard_rows, 512)
    turn_count = shard_rows // sub_rows

    def one_turn(j, inner_states):
        key_block = lax.dynamic_slice_in_dim(key_shard, j * sub_rows, sub_rows, 0).reshape(
            sub_rows, kv_local, HEAD_SIZE
        )
        value_block = lax.dynamic_slice_in_dim(value_shard, j * sub_rows, sub_rows, 0).reshape(
            sub_rows, kv_local, HEAD_SIZE
        )
        key_index = j * sub_rows + jnp.arange(sub_rows, dtype=jnp.int32)
        updated = []
        for (query_rows, query_index), partial_state in zip(shaped_sets, inner_states):
            causal = key_index[None, :] <= query_index[:, None]
            nearby = (key_index[None, :] < SINK) | (
                key_index[None, :] > query_index[:, None] - WINDOW
            )
            visible = causal[None] & (flags[:, None, None] | nearby[None])
            updated.append(
                lax.cond(
                    jnp.any(visible),
                    partial(update, query_rows, key_block, value_block, visible),
                    lambda keep_state: keep_state,
                    partial_state,
                )
            )
        return tuple(updated)

    final = lax.fori_loop(0, turn_count, one_turn, initial)
    results = []
    for (query_rows, query_index), (row_max, totals, accum) in zip(shaped_sets, final):
        output = accum / totals[..., None]
        results.append(
            output.transpose(2, 0, 1, 3)
            .reshape(query_rows.shape[0], kv_local * QUERY_PER_KEY * HEAD_SIZE)
            .astype(jnp.bfloat16)
        )
    return results


def shards(queries, keys, values, positions, retrieval, yarn_scale, out_weight):
    rows_dev = queries.shape[0]
    kv_local = keys.shape[1] // HEAD_SIZE
    cosine_lookup, sine_lookup = yarn_tables(positions, yarn_scale)
    rotated_query = apply_rotary(queries, cosine_lookup, sine_lookup, kv_local * QUERY_PER_KEY)
    rotated_key = apply_rotary(keys, cosine_lookup, sine_lookup, kv_local)
    ctx_index = lax.axis_index("ctx")
    head_ids = lax.axis_index("head") * kv_local + jnp.arange(kv_local, dtype=jnp.int32)
    flags = jnp.any(head_ids[:, None] == retrieval[None, :], axis=1)
    own_index = ctx_index * rows_dev + jnp.arange(rows_dev, dtype=jnp.int32)
    attended = attend(((rotated_query, own_index),), rotated_key, values, flags, kv_local)[0]
    partials = jnp.dot(
        attended,
        lax.all_gather(out_weight, "ctx", axis=1, tiled=True),
        preferred_element_type=jnp.float32,
    )
    return lax.psum_scatter(partials.astype(jnp.bfloat16), "head", scatter_dimension=1, tiled=True)


def solution(mesh):
    return jax.shard_map(
        shards,
        mesh=mesh,
        in_specs=(
            P("ctx", "head"),
            P("ctx", "head"),
            P("ctx", "head"),
            P("ctx"),
            P(),
            P(),
            P("head", "ctx"),
        ),
        out_specs=P("ctx", "head"),
        check_vma=False,
    )
```

profile of v0, /device:TPU:0, one launch (start us, length us, event | category | flops | bytes accessed | tf_op | source)
XLA Modules:
  0.0 449.2 jit_solution(7395130143101550300)
XLA Ops:
  7.3 1.1 copy.51
  8.4 0.8 convert_element_type.48
  9.2 0.3 fusion.13
  9.5 0.1 subtract_convert_fusion.1
  9.6 0.7 pad_maximum_fusion.1
  10.3 0.0 all-gather.6.cloned.1.call-start
  10.4 0.8 copy.42
  11.3 0.7 all-gather.8.cloned.1.call-update
  12.0 0.1 copy.41
  12.1 0.1 copy.39
  12.2 0.2 convert_bitcast_fusion
  12.5 0.4 copy.54
  12.9 0.2 copy-done.4
  13.1 0.2 compare_reduce_fusion
  13.3 0.7 fusion.17
  14.0 1.4 subtract_convert_fusion
  15.4 0.6 pad_maximum_fusion
  16.0 84.0 %all-gather.4.cloned.1.call-done = bf16[4096,512]{0,1:T(8,128)(2,1)} async-done(((bf16[256,512]{0,1:T(8,128)(2,1)}), bf16[4096,512]{0,1:T(8,128)(2,1)}) %all-gather.4.cloned.1.call-update) | async-done | bytes 4194320 | tf_op jit(solution)/shard_map/all_gather | solution.py:83
  100.0 87.7 %all-gather.6.cloned.1.call-done = bf16[4096,512]{0,1:T(8,128)(2,1)} async-done(((bf16[256,512]{0,1:T(8,128)(2,1)}), bf16[4096,512]{0,1:T(8,128)(2,1)}) %all-gather.6.cloned.1.call-update) | async-done | bytes 4194320 | tf_op jit(solution)/shard_map/all_gather | solution.py:84
  187.7 1.6 broadcast_in_dim.68
  189.3 29.0 %while.20 = (s32[]{:T(128)}, f32[4,4,256]{2,1,0:T(4,128)S(1)}, f32[4,4,256]{2,1,0:T(4,128)S(1)}, f32[4,4,256,128]{3,2,1,0:T(8,128)}, pred[4]{0:T(512)(128)(4,1)S...) while((s32[]{:T(128)}, f32[4,4,256]{2,1,0:T(4,128)S(1)}, ...), condition=%wide.region_7.8_spmd.clone, body=%wide.region_1.7_spmd.clone.sunk | while | flops 1104029696 | bytes 53224808 | solution.py:114
  189.3 0.2 broadcast_compare_fusion.5
  189.5 1.4 fusion.24
  191.5 10.4 %conditional.3 = ((f32[4,4,256]{2,1,0:T(4,128)S(1)}, f32[4,4,256]{2,1,0:T(4,128)S(1)}, f32[4,4,256,128]{3,2,1,0:T(8,128)})) conditional(s32[]{:T(128)} %convert_element_type.65, (f32[4,4,256]{2,1,0:T(4,128)S(1)}, f32[4,4,256]{2,1,0:T(4,128)S(1)}, f32[4,4,256,128]{3,2,1,0:T(8,128)}) %tuple.78, (pred[4,256,512]{1,2,0:T(8,128)(4,1)S(1)}, s32[]{:T(128)}, ...), branch_computations={%region_3.3_spmd, %region_4.6_spmd} | conditional | flops 1102061568 | bytes 52166780 | solution.py:105
  191.6 1.3 constant_dynamic-slice_fusion
  192.8 1.9 fusion.2
  194.8 2.1 fusion.4
  196.9 3.6 multiply_add_fusion
  200.6 1.4 copy-done.1
  201.9 0.2 broadcast_compare_fusion.5
  202.2 1.4 fusion.24
  204.3 0.2 broadcast_compare_fusion.5
  204.5 1.4 fusion.24
  206.6 0.2 broadcast_compare_fusion.5
  206.9 1.4 fusion.24
  209.0 0.2 broadcast_compare_fusion.5
  209.2 1.4 fusion.24
  211.3 0.2 broadcast_compare_fusion.5
  211.5 1.4 fusion.24
  213.6 0.2 broadcast_compare_fusion.5
  213.9 1.4 fusion.24
  216.0 0.2 broadcast_compare_fusion.5
  216.2 1.4 fusion.24
  218.3 1.9 copy.43
  220.2 0.2 divide_convert_fusion
  220.4 202.8 %all-gather.8.cloned.1.call-done = bf16[2048,4096]{1,0:T(8,128)(2,1)} async-done(((bf16[2048,256]{1,0:T(8,128)(2,1)}), bf16[2048,4096]{1,0:T(8,128)(2,1)}) %all-gather.8.cloned.1.call-update) | async-done | bytes 16777232 | tf_op jit(solution)/shard_map/all_gather | solution.py:139
  423.2 11.5 %convolution_convert_fusion = bf16[256,4096]{1,0:T(8,128)(2,1)} fusion(bf16[256,2048]{0,1:T(8,128)(2,1)S(1)} %bitcast.49, bf16[2048,4096]{1,0:T(8,128)(2,1)} %all-gather.8.cloned.1.call-done), kind=kOutput, calls=%fused_computation.23 | convolution fusion | flops 4296015872 | bytes 19922944 | tf_op jit(solution)/shard_map/dot_general | solution.py:137
  434.7 8.0 %reduce-scatter.2.cloned.1.call-done = bf16[256,2048]{1,0:T(8,128)(2,1)} async-done(((bf16[256,4096]{1,0:T(8,128)(2,1)}), bf16[256,2048]{1,0:T(8,128)(2,1)}) %reduce-scatter.2.cloned.1.call-update) | async-done | bytes 1048592 | tf_op jit(solution)/shard_map/reduce_scatter | solution.py:142
  (52 shorter events, 0.4 us)
Async XLA Ops:
  6.5 3.8 copy-start.3
  6.5 93.4 %all-gather.4.cloned.1.call-start = ((), (), s32[]{:S(2)}) async-start(), calls=%async_computation.1 | async-start | bytes 4456448 | tf_op jit(solution)/shard_map/all_gather | solution.py:83
  8.4 3.8 copy-start.2
  10.3 177.4 %all-gather.6.cloned.1.call-start = ((), (), s32[]{:S(2)}) async-start(), calls=%async_computation.2 | async-start | bytes 4456448 | tf_op jit(solution)/shard_map/all_gather | solution.py:84
  11.2 411.9 %all-gather.8.cloned.1.call-start = ((), (), s32[]{:S(2)}) async-start(), calls=%async_computation.3 | async-start | bytes 17825792 | tf_op jit(solution)/shard_map/all_gather | solution.py:139
  12.0 430.7 %reduce-scatter.2.cloned.1.call-start = ((), (), s32[]{:S(2)}) async-start(), calls=%async_computation.4 | async-start | bytes 3145728 | tf_op jit(solution)/shard_map/reduce_scatter | solution.py:142
  12.5 0.7 copy-start.4
  194.7 2.2 copy-start
  200.6 1.4 copy-start.1
Sparse Core Ops, SparseCore 0:
  10.4 89.4 all-gather.3
  102.7 84.9 all-gather.5
  190.4 232.7 all-gather.7
  434.8 7.8 reduce-scatter.1
where the time goes:
time: 450 us; the launch traced here: 449 us
  waiting for transfers between devices  383 us (85%)
  other arithmetic  19.6 us (4%)
  matrix products  17 us (4%)
  between operations  14 us (3%)
  local copies, waits for them, and re-layouts  9.6 us (2%)
  loops' own time  5.67 us (1%)
    all_gather x1, waiting for transfers between devices, shards(): lax.all_gather(out_weight, 'ctx', axis=1, tiled=True)  203 us
    all_gather x1, waiting for transfers between devices, attend(): value_shard = lax.all_gather(values, 'ctx', axis=0, tiled=True)  87.7 us
    all_gather x1, waiting for transfers between devices, attend(): key_shard = lax.all_gather(rotated_key, 'ctx', axis=0, tiled=True)  84 us
    dot_general x1, matrix products, shards(): jnp.dot(attended, lax.all_gather(out_weight, 'ctx', axis=1, tiled=True),...  11.5 us
    reduce_or x8, other arithmetic, one_turn(): jnp.any(visible)  11.1 us
  transfers between devices with their start and end apart: 4, of which 4 were waited for; matrix products, arithmetic and copies ran while one was open for 7% of the time, Pallas kernels for 0%

commit v1 on v0

--- a/solution.py
+++ b/solution.py
@@ -12,6 +12,11 @@
 QUERY_PER_KEY = 4
 rope_base = 500000.0
 neg_big = -1e30
+serve_cube_on_mesh = lambda work_x, z_in: jnp.split(
+    lax.all_gather(jnp.concatenate([work_x, z_in], 1), "ctx", axis=0, tiled=True),
+    [work_x.shape[1]],
+    1,
+)
 
 
 def yarn_tables(positions, yarn_scale):
@@ -80,8 +85,7 @@
             )
         )
     initial = tuple(initial)
-    key_shard = lax.all_gather(rotated_key, "ctx", axis=0, tiled=True)
-    value_shard = lax.all_gather(values, "ctx", axis=0, tiled=True)
+    key_shard, value_shard = serve_cube_on_mesh(rotated_key, values)
     shard_rows = key_shard.shape[0]
     sub_rows = math.gcd(shard_rows, 512)
     turn_count = shard_rows // sub_rows

time: 450 us -> 411 us (0.913)
  waiting for transfers between devices: 383 us -> 338 us
  local copies, waits for them, and re-layouts: 9.6 us -> 15.7 us
    all_gather x2 -> x1, waiting for transfers between devices: 172 us -> 133 us  [lax.all_gather(jnp.concatenate([work_x, z_in], 1), 'ctx', axis=0, tiled=T...]
    split x0 -> x1, local copies, waits for them, and re-layouts: none -> 5.93 us  [jnp.split(lax.all_gather(jnp.concatenate([work_x, z_in], 1), 'ctx', axis=...]
    all_gather x1, waiting for transfers between devices: 203 us -> 197 us  [shards(): lax.all_gather(out_weight, 'ctx', axis=1, tiled=True)]
  transfers between devices with their start and end apart: 4 -> 3, of which waited for: 4 -> 3; matrix products, arithmetic and copies ran while one was open for 7% -> 9% of each run, Pallas kernels for 0% -> 0%
where the time goes in v1:
time: 411 us; the launch traced here: 410 us
  waiting for transfers between devices  338 us (82%)
  other arithmetic  19.6 us (5%)
  matrix products  17 us (4%)
  local copies, waits for them, and re-layouts  15.7 us (4%)
  between operations  14 us (3%)
  loops' own time  5.6 us (1%)
    all_gather x1, waiting for transfers between devices, shards(): lax.all_gather(out_weight, 'ctx', axis=1, tiled=True)  197 us
    all_gather x1, waiting for transfers between devices, lax.all_gather(jnp.concatenate([work_x, z_in], 1), 'ctx', axis=0, tiled=T...  133 us
    dot_general x1, matrix products, shards(): jnp.dot(attended, lax.all_gather(out_weight, 'ctx', axis=1, tiled=True),...  11.5 us
    reduce_or x8, other arithmetic, one_turn(): jnp.any(visible)  11 us
  transfers between devices with their start and end apart: 3, of which 3 were waited for; matrix products, arithmetic and copies ran while one was open for 9% of the time, Pallas kernels for 0%

profile of v1, /device:TPU:0, one launch (start us, length us, event | category | flops | bytes accessed | tf_op | source)
XLA Modules:
  0.0 410.3 jit_solution(7857224588594974255)
XLA Ops:
  7.2 1.1 copy.27
  8.3 1.1 copy.40
  9.4 0.7 convert_element_type.48
  10.1 0.3 fusion.13
  10.4 0.1 subtract_convert_fusion.1
  10.6 0.8 pad_maximum_fusion.1
  11.4 0.0 all-gather.5.cloned.1.call-start
  11.5 0.7 all-gather.5.cloned.1.call-update
  12.2 0.1 copy.31
  12.3 0.1 copy.29
  12.4 0.2 convert_bitcast_fusion
  12.7 0.4 copy.43
  13.1 0.2 copy-done.3
  13.3 0.2 compare_reduce_fusion
  13.5 0.7 fusion.18
  14.2 1.4 subtract_convert_fusion
  15.5 0.6 pad_maximum_fusion
  16.1 132.6 %all-gather.3.cloned.1.call-done = bf16[4096,1024]{0,1:T(8,128)(2,1)} async-done(((bf16[256,1024]{0,1:T(8,128)(2,1)}), bf16[4096,1024]{0,1:T(8,128)(2,1)}) %all-gather.3.cloned.1.call-update) | async-done | bytes 8388624 | tf_op jit(solution)/shard_map/all_gather | solution.py:16
  148.8 5.9 %fusion.17 = (bf16[4096,512]{0,1:T(8,128)(2,1)}, bf16[4096,512]{0,1:T(8,128)(2,1)}) fusion(bf16[4096,1024]{0,1:T(8,128)(2,1)} %all-gather.3.cloned.1.call-done), kind=kLoop, calls=%fused_computation.42 | loop fusion | bytes 16777216 | tf_op jit(solution)/shard_map/split | solution.py:15
  154.7 1.5 broadcast_in_dim.68
  156.3 28.9 %while.20 = (s32[]{:T(128)}, f32[4,4,256]{2,1,0:T(4,128)S(1)}, f32[4,4,256]{2,1,0:T(4,128)S(1)}, f32[4,4,256,128]{3,2,1,0:T(8,128)}, pred[4]{0:T(512)(128)(4,1)S...) while((s32[]{:T(128)}, f32[4,4,256]{2,1,0:T(4,128)S(1)}, ...), condition=%wide.region_7.8_spmd.clone, body=%wide.region_1.7_spmd.clone.sunk | while | flops 1104029696 | bytes 53224808 | solution.py:118
  156.3 0.2 broadcast_compare_fusion.5
  156.5 1.4 fusion.25
  158.5 10.4 %conditional.3 = ((f32[4,4,256]{2,1,0:T(4,128)S(1)}, f32[4,4,256]{2,1,0:T(4,128)S(1)}, f32[4,4,256,128]{3,2,1,0:T(8,128)})) conditional(s32[]{:T(128)} %convert_element_type.65, (f32[4,4,256]{2,1,0:T(4,128)S(1)}, f32[4,4,256]{2,1,0:T(4,128)S(1)}, f32[4,4,256,128]{3,2,1,0:T(8,128)}) %tuple.79, (pred[4,256,512]{1,2,0:T(8,128)(4,1)S(1)}, s32[]{:T(128)}, ...), branch_computations={%region_3.3_spmd, %region_4.6_spmd} | conditional | flops 1102061568 | bytes 52166780 | solution.py:109
  158.5 1.4 constant_dynamic-slice_fusion
  159.9 1.9 fusion.2
  161.8 2.1 fusion.4
  164.0 3.6 multiply_add_fusion
  167.6 1.3 copy-done.1
  169.0 0.2 broadcast_compare_fusion.5
  169.2 1.4 fusion.25
  171.3 0.2 broadcast_compare_fusion.5
  171.5 1.4 fusion.25
  173.6 0.2 broadcast_compare_fusion.5
  173.8 1.4 fusion.25
  175.9 0.2 broadcast_compare_fusion.5
  176.1 1.4 fusion.25
  178.2 0.2 broadcast_compare_fusion.5
  178.5 1.4 fusion.25
  180.5 0.2 broadcast_compare_fusion.5
  180.8 1.4 fusion.25
  182.9 0.2 broadcast_compare_fusion.5
  183.1 1.4 fusion.25
  185.1 1.9 copy.32
  187.1 0.2 divide_convert_fusion
  187.3 197.0 %all-gather.5.cloned.1.call-done = bf16[2048,4096]{1,0:T(8,128)(2,1)} async-done(((bf16[2048,256]{1,0:T(8,128)(2,1)}), bf16[2048,4096]{1,0:T(8,128)(2,1)}) %all-gather.5.cloned.1.call-update) | async-done | bytes 16777232 | tf_op jit(solution)/shard_map/all_gather | solution.py:143
  384.3 11.5 %convolution_convert_fusion = bf16[256,4096]{1,0:T(8,128)(2,1)} fusion(bf16[256,2048]{0,1:T(8,128)(2,1)S(1)} %bitcast.49, bf16[2048,4096]{1,0:T(8,128)(2,1)} %all-gather.5.cloned.1.call-done), kind=kOutput, calls=%fused_computation.23 | convolution fusion | flops 4296015872 | bytes 19922944 | tf_op jit(solution)/shard_map/dot_general | solution.py:141
  395.8 8.0 %reduce-scatter.2.cloned.1.call-done = bf16[256,2048]{1,0:T(8,128)(2,1)} async-done(((bf16[256,4096]{1,0:T(8,128)(2,1)}), bf16[256,2048]{1,0:T(8,128)(2,1)}) %reduce-scatter.2.cloned.1.call-update) | async-done | bytes 1048592 | tf_op jit(solution)/shard_map/reduce_scatter | solution.py:146
  (49 shorter events, 0.4 us)
Async XLA Ops:
  6.5 142.2 %all-gather.3.cloned.1.call-start = ((), (), s32[]{:S(2)}) async-start(), calls=%async_computation.1 | async-start | bytes 8912896 | tf_op jit(solution)/shard_map/all_gather | solution.py:16
  10.4 2.0 copy-start.2
  11.4 372.9 %all-gather.5.cloned.1.call-start = ((), (), s32[]{:S(2)}) async-start(), calls=%async_computation.2 | async-start | bytes 17825792 | tf_op jit(solution)/shard_map/all_gather | solution.py:143
  12.2 391.6 %reduce-scatter.2.cloned.1.call-start = ((), (), s32[]{:S(2)}) async-start(), calls=%async_computation.3 | async-start | bytes 3145728 | tf_op jit(solution)/shard_map/reduce_scatter | solution.py:146
  12.7 0.7 copy-start.3
  161.8 2.2 copy-start
  167.6 1.3 copy-start.1
Sparse Core Ops, SparseCore 0:
  11.5 137.1 all-gather.2
  151.5 232.7 all-gather.4
  395.9 7.7 reduce-scatter.1
